TPU v7x, 256 devices: a whole 4x4x8 slice. The times are simulated.
256 devices in a mesh: gx: 8 (over y, core), gy: 32 (over x, z).
Axes of the slice: x: 4, y: 4, z: 8, core: 2. Of those that a mesh axis runs over, the one named last changes fastest.
Arguments:
- inputs: bfloat16 [3072, 7168], P('gy', 'gx'), may hold values from -6 to 6
- query_weight: bfloat16 [7168, 7168], P('gy', 'gx'), may hold values from -0.0625 to 0.0625
- key_weight: bfloat16 [7168, 7168], P('gy', 'gx'), may hold values from -0.0625 to 0.0625
- value_weight: bfloat16 [7168, 7168], P('gy', 'gx'), may hold values from -0.0625 to 0.0625
- adapter_down: bfloat16 [128, 7168], P(None, 'gx'), may hold values from -0.0625 to 0.0625
- adapter_up: bfloat16 [7168, 128], P('gy'), may hold values from -0.5 to 0.5
- prompt_keys: bfloat16 [8, 7168, 2048], P('gx', 'gy'), may hold values from -6 to 6
- prompt_values: bfloat16 [8, 7168, 2048], P('gx', 'gy'), may hold values from -6 to 6
- cache_keys: bfloat16 [64, 7168, 512], P('gx', 'gy'), may hold values from -240 to 240
- cache_values: bfloat16 [64, 7168, 512], P('gx', 'gy'), may hold values from -6 to 6
- cache_lengths: int32 [64], P('gx'), may hold values from 1 to 512, as said below
- parents: int32 [64, 48], P('gx'), may hold values from 0 to 46, as said below
- out_weight: bfloat16 [7168, 3584], P('gy', 'gx'), may hold values from -0.125 to 0.125
Outputs:
- layer_output: bfloat16 [3072, 3584], P('gx', 'gy')
Inputs may be any that keep to these rules, and one draw needn't show every extreme that they name: `parents`: node n's parent is a node below n, node 0 is its own parent, and node 47 hangs from node 46. `cache_lengths`: some request has all 512 positions valid.
All inputs are finite; a program needn't handle non-finite values.
Results may differ from a plain program's by a relative error of at most 0.017.
Values may be sent and summed in bfloat16 or wider, within the bound.
No kernel may reach another device: no remote copies, remote signals or barrier semaphores. Data moves between devices by JAX's collectives and lax.ppermute only.
A program may use at most 128 MiB of HBM per device.

v0:
```python
import math
import jax
import jax.numpy as jnp
import numpy as np
from jax import lax
from jax.sharding import Mesh
from jax.sharding import PartitionSpec as P

HEAD = 224
GY = ("gyx", "gyz")


def contract_rows(left, right):
    return lax.dot_general(
        left, right, (((1,), (1,)), ((), ())), preferred_element_type=jnp.float32
    )


def ancestors(parents):
    node_count = parents.shape[1]
    columns = jnp.arange(node_count, dtype=jnp.int32)
    parent_hot = (parents[:, :, None] == columns[None, None, :]).astype(jnp.float32)
    reached = jnp.minimum(jnp.eye(node_count, dtype=jnp.float32)[None] + parent_hot, 1.0)
    rounds = max(1, math.ceil(math.log2(node_count)))
    for sweep in range(rounds):
        reached = jnp.minimum(
            reached + jnp.einsum("rnm,rmk->rnk", reached, reached, precision=lax.Precision.HIGHEST),
            1.0,
        )
    return reached


def attend(queries, new_keys, new_values, prompt_k, prompt_v, cache_k, cache_v, lengths, parents):
    factor = 1.0 / math.sqrt(queries.shape[-1])
    s_prompt = (
        jnp.einsum("rnhe,hep->rnhp", queries, prompt_k, preferred_element_type=jnp.float32) * factor
    )
    s_cache = (
        jnp.einsum("rnhe,rhec->rnhc", queries, cache_k, preferred_element_type=jnp.float32) * factor
    )
    s_tree = (
        jnp.einsum("rnhe,rmhe->rnhm", queries, new_keys, preferred_element_type=jnp.float32)
        * factor
    )
    usable = jnp.arange(cache_k.shape[-1], dtype=jnp.int32)[None, :] < lengths[:, None]
    s_cache = jnp.where(usable[:, None, None, :], s_cache, -jnp.inf)
    reached = ancestors(parents)
    s_tree = jnp.where(reached[:, :, None, :] > 0.5, s_tree, -jnp.inf)
    largest = jnp.maximum(
        jnp.maximum(
            jnp.max(s_prompt, axis=-1, keepdims=True), jnp.max(s_cache, axis=-1, keepdims=True)
        ),
        jnp.max(s_tree, axis=-1, keepdims=True),
    )
    e_prompt = jnp.exp(s_prompt - largest)
    e_cache = jnp.exp(s_cache - largest)
    e_tree = jnp.exp(s_tree - largest)
    totals = (
        jnp.sum(e_prompt, axis=-1, keepdims=True)
        + jnp.sum(e_cache, axis=-1, keepdims=True)
        + jnp.sum(e_tree, axis=-1, keepdims=True)
    )
    w_prompt = (e_prompt / totals).astype(jnp.bfloat16)
    w_cache = (e_cache / totals).astype(jnp.bfloat16)
    w_tree = (e_tree / totals).astype(jnp.bfloat16)
    result = jnp.einsum("rnhp,hep->rnhe", w_prompt, prompt_v, preferred_element_type=jnp.float32)
    result = result + jnp.einsum(
        "rnhc,rhec->rnhe", w_cache, cache_v, preferred_element_type=jnp.float32
    )
    result = result + jnp.einsum(
        "rnhm,rmhe->rnhe", w_tree, new_values, preferred_element_type=jnp.float32
    )
    return result.astype(jnp.bfloat16)


CHUNKS = 1


def gather_like_all_to_all(block, axis_name):
    count = lax.psum(1, axis_name)
    copies = jnp.broadcast_to(block[None], (count,) + block.shape)
    return lax.all_to_all(copies, axis_name, 0, 0, tiled=True)


def per_device(
    inputs,
    query_weight,
    key_weight,
    value_weight,
    adapter_down,
    adapter_up,
    prompt_keys,
    prompt_values,
    cache_keys,
    cache_values,
    cache_lengths,
    parents,
    out_weight,
):
    along_x = lax.psum(1, "gyx")
    along_z = lax.psum(1, "gyz")
    groups = lax.psum(1, "gx")
    node_count = parents.shape[1]
    head_width = query_weight.shape[0]
    head_count = head_width // HEAD
    per_x = groups // along_x
    columns = out_weight.shape[1]
    every_block = gather_like_all_to_all(out_weight, "gx")
    every_block = every_block.reshape(along_x, per_x, head_width, columns)
    own_block = lax.all_to_all(every_block, "gyx", 0, 0, tiled=True)
    folded = jnp.dot(adapter_up, adapter_down, preferred_element_type=jnp.float32)
    folded = (query_weight.astype(jnp.float32) + folded).astype(jnp.bfloat16)
    weights = jnp.concatenate([folded, key_weight, value_weight], axis=0)
    local = inputs.shape[0]
    rows = local // CHUNKS
    results = []
    for chunk in range(CHUNKS):
        piece = inputs[chunk * rows : (chunk + 1) * rows]
        gathered = lax.all_gather(piece, GY, axis=0, tiled=True)
        if chunk == CHUNKS - 1:
            gathered, own_block, weights = lax.optimization_barrier((gathered, own_block, weights))
        mixture = lax.psum_scatter(
            contract_rows(gathered, weights), "gx", scatter_dimension=0, tiled=True
        )
        queries = mixture[:, :head_width].astype(jnp.bfloat16)
        new_keys = mixture[:, head_width : 2 * head_width].astype(jnp.bfloat16)
        new_values = mixture[:, 2 * head_width :].astype(jnp.bfloat16)
        requests = mixture.shape[0] // node_count
        shaped = (requests, node_count, head_count, HEAD)
        cached = (requests, head_count, HEAD, cache_keys.shape[2])
        attended = attend(
            queries.reshape(shaped),
            new_keys.reshape(shaped),
            new_values.reshape(shaped),
            prompt_keys,
            prompt_values,
            cache_keys[chunk::CHUNKS].reshape(cached),
            cache_values[chunk::CHUNKS].reshape(cached),
            cache_lengths[chunk::CHUNKS],
            parents[chunk::CHUNKS],
        )
        flattened = attended.reshape(requests * node_count, head_width)
        heads_along_x = lax.all_gather(flattened, "gyx", axis=1, tiled=True)
        heads_along_x = heads_along_x.reshape(requests * node_count, along_x, head_width)
        partial_sums = jnp.einsum(
            "txe,xkec->tkc", heads_along_x, own_block, preferred_element_type=jnp.float32
        )
        pieces = partial_sums.astype(jnp.bfloat16).reshape(requests * node_count, along_z, -1)
        landed = lax.all_to_all(pieces, "gyz", 1, 1, tiled=True)
        out = jnp.sum(landed.astype(jnp.float32), axis=1).astype(jnp.bfloat16)
        results.append(out.reshape(requests, node_count, -1))
    stacked = jnp.stack(results, axis=1)
    return stacked.reshape(-1, stacked.shape[-1])


def split_mesh(mesh):
    devices = mesh.devices
    along_x = len({d.coords[0] for d in devices[0]})
    shape = (devices.shape[0], along_x, devices.shape[1] // along_x)
    return Mesh(devices.reshape(shape), ("gx",) + GY)


def solution(mesh):
    placed = (
        P(GY, "gx"),
        P(GY, "gx"),
        P(GY, "gx"),
        P(GY, "gx"),
        P(None, "gx"),
        P(GY, None),
        P("gx", GY, None),
        P("gx", GY, None),
        P("gx", GY, None),
        P("gx", GY, None),
        P("gx"),
        P("gx", None),
        P(GY, "gx"),
    )
    return jax.shard_map(
        per_device, mesh=split_mesh(mesh), in_specs=placed, out_specs=P("gx", GY), check_vma=False
    )
```

profile of v0, /device:TPU:8, one launch (start us, length us, event | category | flops | bytes accessed | tf_op | source)
XLA Modules:
  0.0 218.0 jit_solution(15827629615756202001)
XLA Ops:
  6.5 0.7 all-gather.2.cloned.1.call-update
  7.3 1.1 broadcast_in_dim.17
  8.4 28.4 %all_to_all.15 = bf16[8,224,448]{2,1,0:T(8,128)(2,1)} all-to-all(bf16[8,224,448]{2,1,0:T(8,128)(2,1)S(1)} %broadcast_in_dim.17), channel_id=1, replica_groups=mesh['gx'=8,'gyx'=4,'gyz'=8] {'gx'}, dimensions={0} | all-to-all | bytes 3211264 | tf_op jit(solution)/shard_map/all_to_all | solution.py:82
  36.8 4.5 %all-to-all-start.1 = ((bf16[4,2,224,448]{3,2,1,0:T(8,128)(2,1)}), bf16[4,2,224,448]{3,2,1,0:T(8,128)(2,1)}, u32[]{:S(2)}, u32[]{:S(2)}) async-start(bf16[4,2,224,448]{3,2,1,0:T(8,128)(2,1)} %bitcast.120), calls=%async_computation.1 | async-start | bytes 3670016 | tf_op jit(solution)/shard_map/all_to_all | solution.py:110
  41.7 1.1 pad_maximum_fusion
  42.8 22.0 %all-to-all-done.1 = bf16[4,2,224,448]{3,2,1,0:T(8,128)(2,1)} async-done(((bf16[4,2,224,448]{3,2,1,0:T(8,128)(2,1)}), bf16[4,2,224,448]{3,2,1,0:T(8,128)(2,1)}, u32[]{:S(2)}, u32[]{:S(2)}) %all-to-all-start.1) | async-done | bytes 1605664 | tf_op jit(solution)/shard_map/all_to_all | solution.py:110
  64.8 34.1 %all-gather.2.cloned.1.call-done = bf16[3072,896]{1,0:T(8,128)(2,1)} async-done(((bf16[96,896]{1,0:T(8,128)(2,1)}), bf16[3072,896]{1,0:T(8,128)(2,1)}) %all-gather.2.cloned.1.call-update) | async-done | bytes 5505040 | tf_op jit(solution)/shard_map/all_gather | solution.py:119
  98.9 9.2 %fusion.44 = f32[3072,672]{0,1:T(8,128)} fusion(bf16[3072,896]{1,0:T(8,128)(2,1)} %all-gather.2.cloned.1.call-done, bf16[672,896]{1,0:T(8,128)(2,1)S(1)} %pad_maximum_fusion), kind=kOutput, calls=%fused_computation.68 | convolution fusion | flops 3699376128 | bytes 14966784 | tf_op jit(solution)/shard_map/dot_general | solution.py:14
  108.1 0.6 copy-done.8
  108.7 0.4 fusion.15
  109.1 0.3 fusion.16
  109.7 0.3 fusion.18
  110.4 0.3 fusion.24
  110.8 45.9 %reduce-scatter.2.cloned.1.call-done = f32[384,672]{0,1:T(8,128)} async-done(((f32[3072,672]{0,1:T(8,128)}), f32[384,672]{0,1:T(8,128)}) %reduce-scatter.2.cloned.1.call-update) | async-done | bytes 1032208 | tf_op jit(solution)/shard_map/reduce_scatter | solution.py:122
  156.7 1.3 convert.6
  158.4 1.8 bitcast_reduce_fusion
  160.4 0.5 fusion.43
  161.3 0.6 fusion.1
  162.1 3.0 %fusion.9 = f32[8,48,1,224]{3,1,0,2:T(8,128)S(1)} fusion(f32[8,48]{1,0:T(8,128)S(1)} %add_add_fusion, f32[8,48]{1,0:T(8,128)S(1)} %maximum_maximum_fusion, f32[8,48,2048]{2,1,0:T(8,128)} %copy-done.1, bf16[1,224,2048]{2,1,0:T(8,128)(2,1)} %param.20), kind=kOutput, calls=%fused_computation.17 | convolution fusion | flops 354680832 | bytes 4410368 | tf_op jit(solution)/shard_map/rnhp,hep->rnhe/dot_general | solution.py:66
  165.3 0.7 fusion.14
  166.2 14.4 %all_gather.7 = bf16[384,896]{0,1:T(8,128)(2,1)S(1)} all-gather(bf16[384,224]{0,1:T(8,128)(2,1)S(1)} %copy.49), channel_id=1, replica_groups=mesh['gx'=8,'gyx'=4,'gyz'=8] {'gyx'}, dimensions={1}, use_global_device_ids=true | all-gather | bytes 860160 | tf_op jit(solution)/shard_map/all_gather | solution.py:143
  180.6 2.6 %fusion.4 = bf16[384,2,448]{0,2,1:T(8,128)(2,1)S(1)} fusion(bf16[384,4,224,1]{0,2,3,1:T(8,128)(2,1)S(1)} %bitcast.126, bf16[4,2,224,448]{3,2,1,0:T(8,128)(2,1)} %all-to-all-done.1), kind=kOutput, calls=%fused_computation.9 | convolution fusion | flops 616906752 | bytes 2981888 | tf_op jit(solution)/shard_map/txe,xkec->tkc/dot_general | solution.py:145
  183.2 27.2 %all_to_all.16 = bf16[384,8,112]{0,2,1:T(8,128)(2,1)S(1)} all-to-all(bf16[384,8,112]{0,2,1:T(8,128)(2,1)S(1)} %bitcast.125), channel_id=1, replica_groups=mesh['gx'=8,'gyx'=4,'gyz'=8] {'gyz'}, dimensions={1} | all-to-all | bytes 1376256 | tf_op jit(solution)/shard_map/all_to_all | solution.py:149
  210.4 0.7 reduce_sum.42
  (36 shorter events, 2.5 us)
Async XLA Ops:
  6.5 153.9 %copy-start = (bf16[8,224,512]{2,1,0:T(8,128)(2,1)S(1)}, bf16[8,224,512]{2,1,0:T(8,128)(2,1)}, u32[]{:S(2)}) copy-start(bf16[8,224,512]{2,1,0:T(8,128)(2,1)} %param.21) | copy-start | bytes 5505028
  6.5 92.3 %all-gather.2.cloned.1.call-start = ((), (), s32[]{:S(2)}) async-start(), calls=%async_computation.4 | async-start | bytes 5677056 | tf_op jit(solution)/shard_map/all_gather | solution.py:119
  36.8 4.6 %copy-start.3 = (bf16[224,896]{1,0:T(8,128)(2,1)S(1)}, bf16[224,896]{1,0:T(8,128)(2,1)}, u32[]{:S(2)}) copy-start(bf16[224,896]{1,0:T(8,128)(2,1)} %param.14) | copy-start | bytes 1204228
  36.8 4.6 %copy-start.4 = (bf16[128,896]{1,0:T(8,128)(2,1)S(1)}, bf16[128,896]{1,0:T(8,128)(2,1)}, u32[]{:S(2)}) copy-start(bf16[128,896]{1,0:T(8,128)(2,1)} %param.17) | copy-start | bytes 688132
  36.8 4.6 %copy-start.5 = (bf16[224,128]{1,0:T(8,128)(2,1)S(1)}, bf16[224,128]{1,0:T(8,128)(2,1)}, u32[]{:S(2)}) copy-start(bf16[224,128]{1,0:T(8,128)(2,1)} %param.18) | copy-start | bytes 172036
  36.8 4.9 %copy-start.2 = (bf16[224,896]{1,0:T(8,128)(2,1)S(1)}, bf16[224,896]{1,0:T(8,128)(2,1)}, u32[]{:S(2)}) copy-start(bf16[224,896]{1,0:T(8,128)(2,1)} %param.16) | copy-start | bytes 1204228
  36.8 28.0 %all-to-all-start.1 = ((bf16[4,2,224,448]{3,2,1,0:T(8,128)(2,1)}), bf16[4,2,224,448]{3,2,1,0:T(8,128)(2,1)}, u32[]{:S(2)}, u32[]{:S(2)}) async-start(bf16[4,2,224,448]{3,2,1,0:T(8,128)(2,1)} %bitcast.120), calls=%async_computation.1 | async-start | bytes 3670016 | tf_op jit(solution)/shard_map/all_to_all | solution.py:110
  41.3 115.4 %reduce-scatter.2.cloned.1.call-start = ((), (), s32[]{:S(2)}) async-start(), calls=%async_computation.5 | async-start | bytes 9289728 | tf_op jit(solution)/shard_map/reduce_scatter | solution.py:122
  108.0 0.7 copy-start.8
  108.1 2.6 %copy-start.6 = (s32[8]{0:T(128)S(1)}, s32[8]{0:T(128)}, u32[]{:S(2)}) copy-start(s32[8]{0:T(128)} %param.23) | copy-start | bytes 100
  160.2 1.7 copy-start.1
  162.0 3.2 %copy-start.7 = (bf16[8,224,512]{2,1,0:T(8,128)(2,1)S(1)}, bf16[8,224,512]{2,1,0:T(8,128)(2,1)}, u32[]{:S(2)}) copy-start(bf16[8,224,512]{2,1,0:T(8,128)(2,1)} %param.22) | copy-start | bytes 5505028
Sparse Core Ops, SparseCore 0:
  9.9 88.9 all-gather.1
  108.2 48.4 reduce-scatter.1
where the time goes:
time: 218 us
  waiting for transfers between devices  103 us (47%)
  blocking collectives  70 us (32%)
  matrix products  20.5 us (9%)
  between operations  13.7 us (6%)
  starting transfers between devices  4.58 us (2%)
  other arithmetic  4.07 us (2%)
  local copies, waits for them, and re-layouts  2.42 us (1%)
    reduce_scatter x1, waiting for transfers between devices, per_device(): lax.psum_scatter(contract_rows(gathered, weights), 'gx', scatter_dimensio...  45.9 us
    all_gather x1, waiting for transfers between devices, per_device(): gathered = lax.all_gather(piece, GY, axis=0, tiled=True)  34.1 us
    all_to_all x1, blocking collectives, gather_like_all_to_all(): return lax.all_to_all(copies, axis_name, 0, 0, tiled=True)  28.4 us
    all_to_all x1, blocking collectives, per_device(): landed = lax.all_to_all(pieces, 'gyz', 1, 1, tiled=True)  27.2 us
    all_to_all x1, waiting for transfers between devices, per_device(): own_block = lax.all_to_all(every_block, 'gyx', 0, 0, tiled=True)  22 us
    all_gather x1, blocking collectives, per_device(): heads_along_x = lax.all_gather(flattened, 'gyx', axis=1, tiled=True)  14.4 us
    dot_general x1, matrix products, contract_rows(): lax.dot_general(left, right, (((1,), (1,)), ((), ())), preferred_element_...  9.16 us
    all_to_all x1, starting transfers between devices, per_device(): own_block = lax.all_to_all(every_block, 'gyx', 0, 0, tiled=True)  4.54 us
  transfers between devices with their start and end apart: 3, of which 3 were waited for; matrix products, arithmetic and copies ran while one was open for 2% of the time, Pallas kernels for 0%

commit v1 on v0

--- a/solution.py
+++ b/solution.py
@@ -1,3 +1,4 @@
+import functools
 import math
 import jax
 import jax.numpy as jnp
@@ -8,6 +9,17 @@
 
 HEAD = 224
 GY = ("gyx", "gyz")
+
+
+def strings_turn(body, group_axis):
+    even = jnp.stack(lax.axis_size(group_axis) * [body])
+    arr_next = jnp.concatenate(
+        lax.all_to_all(even, axis_name=group_axis, split_axis=0, concat_axis=0), axis=0
+    )
+    return arr_next
+
+
+register_packet = functools.partial(strings_turn, group_axis=GY)
 
 
 def contract_rows(left, right):
@@ -116,7 +128,7 @@
     results = []
     for chunk in range(CHUNKS):
         piece = inputs[chunk * rows : (chunk + 1) * rows]
-        gathered = lax.all_gather(piece, GY, axis=0, tiled=True)
+        gathered = register_packet(piece)
         if chunk == CHUNKS - 1:
             gathered, own_block, weights = lax.optimization_barrier((gathered, own_block, weights))
         mixture = lax.psum_scatter(

time: 218 us -> 319 us (1.46)
  waiting for transfers between devices: 103 us -> 168 us
  blocking collectives: 70 us -> 96.9 us
  starting transfers between devices: 4.58 us -> 9.76 us
    all_to_all x1, waiting for transfers between devices: 22 us -> 120 us  [strings_turn(): lax.all_to_all(even, axis_name=group_axis, split_axis=0, concat_axis=0)]
    all_gather x1 -> x0, waiting for transfers between devices: 34.1 us -> none  [per_device(): gathered = lax.all_gather(piece, GY, axis=0, tiled=True)]
    all_to_all x0 -> x1, blocking collectives: none -> 27.5 us  [per_device(): own_block = lax.all_to_all(every_block, 'gyx', 0, 0, tiled=True)]
    all_to_all x1, starting transfers between devices: 4.54 us -> 9.72 us  [strings_turn(): lax.all_to_all(even, axis_name=group_axis, split_axis=0, concat_axis=0)]
  transfers between devices with their start and end apart: 3 -> 2, of which waited for: 3 -> 2; matrix products, arithmetic and copies ran while one was open for 2% -> 1% of each run, Pallas kernels for 0% -> 0%
where the time goes in v1:
time: 319 us; the launch traced here: 318 us
  waiting for transfers between devices  168 us (53%)
  blocking collectives  96.9 us (30%)
  matrix products  20.5 us (6%)
  between operations  13.7 us (4%)
  starting transfers between devices  9.76 us (3%)
  local copies, waits for them, and re-layouts  5.34 us (2%)
  other arithmetic  4.07 us (1%)
    all_to_all x1, waiting for transfers between devices, strings_turn(): lax.all_to_all(even, axis_name=group_axis, split_axis=0, concat_axis=0)  120 us
    reduce_scatter x1, waiting for transfers between devices, per_device(): lax.psum_scatter(contract_rows(gathered, weights), 'gx', scatter_dimensio...  47.9 us
    all_to_all x1, blocking collectives, gather_like_all_to_all(): return lax.all_to_all(copies, axis_name, 0, 0, tiled=True)  27.8 us
    all_to_all x1, blocking collectives, per_device(): own_block = lax.all_to_all(every_block, 'gyx', 0, 0, tiled=True)  27.5 us
    all_to_all x1, blocking collectives, per_device(): landed = lax.all_to_all(pieces, 'gyz', 1, 1, tiled=True)  27.2 us
    all_gather x1, blocking collectives, per_device(): heads_along_x = lax.all_gather(flattened, 'gyx', axis=1, tiled=True)  14.4 us
    all_to_all x1, starting transfers between devices, strings_turn(): lax.all_to_all(even, axis_name=group_axis, split_axis=0, concat_axis=0)  9.72 us
    dot_general x1, matrix products, contract_rows(): lax.dot_general(left, right, (((1,), (1,)), ((), ())), preferred_element_...  9.16 us
  transfers between devices with their start and end apart: 2, of which 2 were waited for; matrix products, arithmetic and copies ran while one was open for 1% of the time, Pallas kernels for 0%

profile of v1, /device:TPU:8, one launch (start us, length us, event | category | flops | bytes accessed | tf_op | source)
XLA Modules:
  0.0 318.2 jit_solution(16721648648887420189)
XLA Ops:
  6.5 1.2 broadcast_in_dim.17
  7.8 27.8 %all_to_all.20 = bf16[8,224,448]{2,1,0:T(8,128)(2,1)S(1)} all-to-all(bf16[8,224,448]{2,1,0:T(8,128)(2,1)S(1)} %broadcast_in_dim.17), channel_id=1, replica_groups=mesh['gx'=8,'gyx'=4,'gyz'=8] {'gx'}, dimensions={0} | all-to-all | bytes 3211264 | tf_op jit(solution)/shard_map/all_to_all | solution.py:94
  35.6 27.5 %all_to_all.21 = bf16[4,2,224,448]{3,2,1,0:T(8,128)(2,1)} all-to-all(bf16[4,2,224,448]{3,2,1,0:T(8,128)(2,1)S(1)} %bitcast.121), channel_id=1, replica_groups=mesh['gx'=8,'gyx'=4,'gyz'=8] {'gyx'}, dimensions={0} | all-to-all | bytes 3211264 | tf_op jit(solution)/shard_map/all_to_all | solution.py:122
  63.1 2.8 stack.2
  65.9 9.7 %all-to-all-start = ((bf16[32,96,896]{2,1,0:T(8,128)(2,1)}), bf16[32,96,896]{2,1,0:T(8,128)(2,1)}, u32[]{:S(2)}, u32[]{:S(2)}) async-start(bf16[32,96,896]{2,1,0:T(8,128)(2,1)} %stack.2), calls=%async_computation | async-start | bytes 11010048 | tf_op jit(solution)/shard_map/all_to_all | solution.py:17
  76.0 1.1 pad_maximum_fusion
  77.1 120.1 %all-to-all-done = bf16[32,96,896]{2,1,0:T(8,128)(2,1)} async-done(((bf16[32,96,896]{2,1,0:T(8,128)(2,1)}), bf16[32,96,896]{2,1,0:T(8,128)(2,1)}, u32[]{:S(2)}, u32[]{:S(2)}) %all-to-all-start) | async-done | bytes 5505056 | tf_op jit(solution)/shard_map/all_to_all | solution.py:17
  197.2 9.2 %fusion.44 = f32[3072,672]{0,1:T(8,128)} fusion(bf16[3072,896]{1,0:T(8,128)(2,1)} %bitcast, bf16[672,896]{1,0:T(8,128)(2,1)S(1)} %pad_maximum_fusion), kind=kOutput, calls=%fused_computation.68 | convolution fusion | flops 3699376128 | bytes 14966784 | tf_op jit(solution)/shard_map/dot_general | solution.py:26
  206.4 0.6 copy-done.9
  207.0 0.4 fusion.15
  207.4 0.3 fusion.16
  208.0 0.3 fusion.18
  208.7 0.3 fusion.24
  209.1 47.9 %reduce-scatter.2.cloned.1.call-done = f32[384,672]{0,1:T(8,128)} async-done(((f32[3072,672]{0,1:T(8,128)}), f32[384,672]{0,1:T(8,128)}) %reduce-scatter.2.cloned.1.call-update) | async-done | bytes 1032208 | tf_op jit(solution)/shard_map/reduce_scatter | solution.py:134
  257.0 1.3 convert.6
  258.6 1.8 bitcast_reduce_fusion
  260.7 0.5 fusion.43
  261.5 0.6 fusion.1
  262.3 3.0 fusion.9
  265.5 0.7 fusion.14
  266.4 14.4 %all_gather.3 = bf16[384,896]{0,1:T(8,128)(2,1)S(1)} all-gather(bf16[384,224]{0,1:T(8,128)(2,1)S(1)} %copy.49), channel_id=1, replica_groups=mesh['gx'=8,'gyx'=4,'gyz'=8] {'gyx'}, dimensions={1}, use_global_device_ids=true | all-gather | bytes 860160 | tf_op jit(solution)/shard_map/all_gather | solution.py:155
  280.8 2.6 fusion.4
  283.5 27.2 %all_to_all.22 = bf16[384,8,112]{0,2,1:T(8,128)(2,1)S(1)} all-to-all(bf16[384,8,112]{0,2,1:T(8,128)(2,1)S(1)} %bitcast.126), channel_id=1, replica_groups=mesh['gx'=8,'gyx'=4,'gyz'=8] {'gyz'}, dimensions={1} | all-to-all | bytes 1376256 | tf_op jit(solution)/shard_map/all_to_all | solution.py:161
  310.7 0.7 reduce_sum.42
  (37 shorter events, 2.5 us)
Async XLA Ops:
  6.5 254.1 %copy-start = (bf16[8,224,512]{2,1,0:T(8,128)(2,1)S(1)}, bf16[8,224,512]{2,1,0:T(8,128)(2,1)}, u32[]{:S(2)}) copy-start(bf16[8,224,512]{2,1,0:T(8,128)(2,1)} %param.21) | copy-start | bytes 5505028
  35.6 27.5 %copy-start.5 = (bf16[96,896]{1,0:T(8,128)(2,1)S(1)}, bf16[96,896]{1,0:T(8,128)(2,1)}, u32[]{:S(2)}) copy-start(bf16[96,896]{1,0:T(8,128)(2,1)} %param.13) | copy-start | bytes 516100
  65.9 9.8 %copy-start.3 = (bf16[224,896]{1,0:T(8,128)(2,1)S(1)}, bf16[224,896]{1,0:T(8,128)(2,1)}, u32[]{:S(2)}) copy-start(bf16[224,896]{1,0:T(8,128)(2,1)} %param.14) | copy-start | bytes 1204228
  65.9 9.8 %copy-start.4 = (bf16[128,896]{1,0:T(8,128)(2,1)S(1)}, bf16[128,896]{1,0:T(8,128)(2,1)}, u32[]{:S(2)}) copy-start(bf16[128,896]{1,0:T(8,128)(2,1)} %param.17) | copy-start | bytes 688132
  65.9 9.8 %copy-start.6 = (bf16[224,128]{1,0:T(8,128)(2,1)S(1)}, bf16[224,128]{1,0:T(8,128)(2,1)}, u32[]{:S(2)}) copy-start(bf16[224,128]{1,0:T(8,128)(2,1)} %param.18) | copy-start | bytes 172036
  65.9 10.1 %copy-start.2 = (bf16[224,896]{1,0:T(8,128)(2,1)S(1)}, bf16[224,896]{1,0:T(8,128)(2,1)}, u32[]{:S(2)}) copy-start(bf16[224,896]{1,0:T(8,128)(2,1)} %param.16) | copy-start | bytes 1204228
  65.9 131.3 %all-to-all-start = ((bf16[32,96,896]{2,1,0:T(8,128)(2,1)}), bf16[32,96,896]{2,1,0:T(8,128)(2,1)}, u32[]{:S(2)}, u32[]{:S(2)}) async-start(bf16[32,96,896]{2,1,0:T(8,128)(2,1)} %stack.2), calls=%async_computation | async-start | bytes 11010048 | tf_op jit(solution)/shard_map/all_to_all | solution.py:17
  75.6 181.3 %reduce-scatter.2.cloned.1.call-start = ((), (), s32[]{:S(2)}) async-start(), calls=%async_computation.5 | async-start | bytes 9289728 | tf_op jit(solution)/shard_map/reduce_scatter | solution.py:134
  206.3 0.7 copy-start.9
  206.4 2.6 copy-start.7
  260.4 1.7 copy-start.1
  262.3 3.2 %copy-start.8 = (bf16[8,224,512]{2,1,0:T(8,128)(2,1)S(1)}, bf16[8,224,512]{2,1,0:T(8,128)(2,1)}, u32[]{:S(2)}) copy-start(bf16[8,224,512]{2,1,0:T(8,128)(2,1)} %param.22) | copy-start | bytes 5505028
Sparse Core Ops, SparseCore 0:
  206.5 50.4 reduce-scatter.1
